TPU v7x, 32 devices: a whole 2x2x4 slice. The times are simulated.
32 devices in a mesh: grp: 2 (over y), seq: 4 (over z), kvh: 2 (over x), sub: 2 (over core).
Axes of the slice: x: 2, y: 2, z: 4, core: 2. Of those that a mesh axis runs over, the one named last changes fastest.
Arguments:
- tokens: bfloat16 [4096, 4096], P(('grp', 'seq'), ('kvh', 'sub')), parts along dimension 0, may hold values from -6 to 6
- norm_gain: float32 [4096], replicated, may hold values from 0.5 to 1.5
- w_query: bfloat16 [4096, 8, 512], P(None, 'kvh', 'sub')
- w_key: bfloat16 [4096, 8, 128], P('sub', 'kvh')
- w_value: bfloat16 [4096, 8, 128], P('sub', 'kvh'), may hold values from -0.09375 to 0.09375
- links: int32 [3, 8], replicated, may hold values from 0 to 7, as said below
Outputs:
- attended: bfloat16 [4096, 8, 512], P(('grp', 'seq'), 'kvh', 'sub'), parts along dimension 0
- gram: float32 [8192, 4096], P(('grp', 'seq'), ('kvh', 'sub')), parts along dimension 0
There are 2 independent parts, one for each index of `grp`. A program takes and returns all parts, laid end to end along the dimension named above; an argument that names none is the same for every part. Nothing has to cross between parts.
Inputs may be any that keep to these rules, and one draw needn't show every extreme that they name: links[b, i] is either i or i xor 2 ** b; the pattern is symmetric: block i names its section-b partner exactly when that partner names i; block 0 names its partner at every section.
All inputs are finite; a program needn't handle non-finite values.
Results may differ from a plain program's by a relative error of at most 0.0095.
Values may be sent and summed in bfloat16 or wider, within the bound.
No kernel may reach another device: no remote copies, remote signals or barrier semaphores. Data moves between devices by JAX's collectives and lax.ppermute only.
A program may use at most 128 MiB of HBM per device.

v0:
```python
import math

import jax
import jax.numpy as jnp
from jax import lax
from jax.sharding import PartitionSpec as P

rope_base = 500000.0


def from_partner(block, axis, bit):
    count = lax.axis_size(axis)
    route = []
    for low in range(count):
        high = low | 1 << bit
        if high != low and high < count:
            route += [(low, high), (high, low)]
    return lax.ppermute(block, axis, route)


def rotate(vectors, positions):
    width = vectors.shape[-1]
    half = width // 2
    inverse = jnp.exp(jnp.arange(half, dtype=jnp.float32) * (-2.0 * math.log(rope_base) / width))
    angles = positions.astype(jnp.float32)[:, None] * inverse[None, :]
    shape = (angles.shape[0],) + (1,) * (vectors.ndim - 2) + (half,)
    cosine = jnp.cos(angles).reshape(shape)
    sine = jnp.sin(angles).reshape(shape)
    first = vectors[..., :half]
    second = vectors[..., half:]
    return jnp.concatenate(
        [first * cosine - second * sine, second * cosine + first * sine], axis=-1
    )


def body(tokens, norm_gain, w_query, w_key, w_value, links):
    gathered = lax.all_gather(tokens, ("kvh", "sub"), axis=1, tiled=True)
    widened = gathered.astype(jnp.float32)
    mean_square = jnp.mean(widened * widened, axis=-1, keepdims=True)
    normed = (widened * lax.rsqrt(mean_square + 1e-05) * norm_gain).astype(jnp.bfloat16)
    row_count = normed.shape[0]
    block_len = row_count // 2
    width = normed.shape[1]
    seq_index = lax.axis_index("seq")
    local_rows = jnp.arange(row_count, dtype=jnp.int32)
    positions = seq_index * row_count + local_rows
    head_size = w_key.shape[2]
    local_groups = w_key.shape[1]
    per_group = w_query.shape[2] // head_size
    queries = jnp.einsum("td,dgc->tgc", normed, w_query, preferred_element_type=jnp.float32)
    queries = rotate(
        queries.reshape(row_count, local_groups, per_group, head_size), positions
    ).astype(jnp.bfloat16)
    key_more = jnp.einsum(
        "td,dgh->tgh",
        normed,
        lax.all_gather(w_key, "sub", axis=0, tiled=True),
        preferred_element_type=jnp.float32,
    )
    value_more = jnp.einsum(
        "td,dgh->tgh",
        normed,
        lax.all_gather(w_value, "sub", axis=0, tiled=True),
        preferred_element_type=jnp.float32,
    )
    keys = rotate(key_more, positions).astype(jnp.bfloat16)
    values = value_more.astype(jnp.bfloat16)
    block_ids = seq_index * 2 + jnp.arange(2, dtype=jnp.int32)
    query_block = local_rows // block_len
    scale = 1.0 / math.sqrt(head_size)
    scores = jnp.einsum("tgrh,ugh->grtu", queries, keys, preferred_element_type=jnp.float32) * scale
    near_linked = lax.dynamic_slice_in_dim(links[0], seq_index * 2, 2) != block_ids
    same_block = query_block[:, None] == query_block[None, :]
    causal = same_block & (local_rows[None, :] <= local_rows[:, None])
    across = ~same_block & near_linked[query_block][:, None]
    allowed = causal | across
    scores = jnp.where(allowed[None, None], scores, -jnp.inf)
    running_max = jnp.max(scores, axis=-1)
    weights = jnp.exp(scores - running_max[..., None])
    total = jnp.sum(weights, axis=-1)
    accum = jnp.einsum(
        "grtu,ugh->tgrh", weights.astype(jnp.bfloat16), values, preferred_element_type=jnp.float32
    )
    query_pairs = queries.reshape(2, block_len, local_groups, per_group, head_size)
    for section in range(1, lax.axis_size("seq").bit_length()):
        far_keys, far_values = from_partner((keys, values), "seq", section - 1)
        far_keys = far_keys.reshape(2, block_len, local_groups, head_size)
        far_values = far_values.reshape(2, block_len, local_groups, head_size)
        linked = lax.dynamic_slice_in_dim(links[section], seq_index * 2, 2) != block_ids
        offset = jnp.where(linked, 0.0, -1e30).astype(jnp.float32)[query_block]
        far_scores = jnp.einsum(
            "jtgrh,jugh->grjtu", query_pairs, far_keys, preferred_element_type=jnp.float32
        )
        far_scores = (
            far_scores.reshape(local_groups, per_group, row_count, block_len) * scale
            + offset[None, None, :, None]
        )
        new_max = jnp.maximum(running_max, jnp.max(far_scores, axis=-1))
        shrink = jnp.exp(running_max - new_max)
        far_weights = jnp.exp(far_scores - new_max[..., None])
        total = total * shrink + jnp.sum(far_weights, axis=-1)
        paired = far_weights.astype(jnp.bfloat16).reshape(
            local_groups, per_group, 2, block_len, block_len
        )
        far_sum = jnp.einsum(
            "grjtu,jugh->jtgrh", paired, far_values, preferred_element_type=jnp.float32
        )
        far_sum = far_sum.reshape(row_count, local_groups, per_group, head_size)
        accum = accum * jnp.transpose(shrink, (2, 0, 1))[..., None] + far_sum
        running_max = new_max
    attended = (accum / jnp.transpose(total, (2, 0, 1))[..., None]).astype(jnp.bfloat16)
    attended = attended.reshape(row_count, local_groups, per_group * head_size)
    tile_count = lax.axis_size("kvh") * lax.axis_size("sub")
    tile_cols = width // tile_count
    owner_index = lax.axis_index("kvh") * lax.axis_size("sub") + lax.axis_index("sub")
    owned = lax.dynamic_slice_in_dim(normed, owner_index * tile_cols, tile_cols, 1)
    seq_count = lax.axis_size("seq")
    inverse_count = 1.0 / (row_count * seq_count)
    gram_tile = lax.psum_scatter(
        (
            jnp.einsum("tc,tr->cr", normed, owned, preferred_element_type=jnp.float32)
            * inverse_count
        ).astype(jnp.bfloat16),
        "seq",
        scatter_dimension=0,
        tiled=True,
    ).astype(jnp.float32)
    return (attended, gram_tile)


def solution(mesh):
    placed = (
        P(("grp", "seq"), ("kvh", "sub")),
        P(),
        P(None, "kvh", "sub"),
        P("sub", "kvh", None),
        P("sub", "kvh", None),
        P(),
    )
    return jax.shard_map(
        body,
        mesh=mesh,
        in_specs=placed,
        out_specs=(P(("grp", "seq"), "kvh", "sub"), P(("grp", "seq"), ("kvh", "sub"))),
        check_vma=False,
    )
```

profile of v0, /device:TPU:0, one launch (start us, length us, event | category | flops | bytes accessed | tf_op | source)
XLA Modules:
  0.0 270.0 jit_solution(4418771752786524630)
XLA Ops:
  8.0 4.3 %copy.31 = bf16[2048,4,128]{0,2,1:T(8,128)(2,1)} copy(bf16[2048,4,128]{2,1,0:T(4,128)(2,1)} %param.9) | data formatting | bytes 4194304 | tf_op args[3]
  12.4 1.6 copy.30
  14.1 32.7 %all-gather.4.cloned.1.call-done = bf16[512,4096]{1,0:T(8,128)(2,1)} async-done(((bf16[512,1024]{1,0:T(8,128)(2,1)}), bf16[512,4096]{1,0:T(8,128)(2,1)}) %all-gather.4.cloned.1.call-update) | async-done | bytes 4194320 | tf_op jit(solution)/shard_map/all_gather | solution.py:37
  46.8 3.2 %fusion = f32[512]{0:T(512)S(1)} fusion(bf16[512,4096]{1,0:T(8,128)(2,1)} %all-gather.4.cloned.1.call-done), kind=kLoop, calls=%fused_computation.3 | loop fusion | flops 6290944 | bytes 4196352 | tf_op jit(solution)/shard_map/reduce_sum | solution.py:39
  50.2 1.6 fusion.2
  51.8 2.0 copy-done.2
  53.9 7.0 %multiply_convert_fusion = bf16[4096,1024]{1,0:T(8,128)(2,1)} fusion(bf16[512,4096]{1,0:T(8,128)(2,1)S(1)} %fusion.2, s32[]{:T(128)S(6)} %select_n.69), kind=kOutput, calls=%fused_computation | convolution fusion | flops 4303355904 | bytes 13631492 | tf_op jit(solution)/shard_map/tc,tr->cr/dot_general | solution.py:121
  62.4 1.3 select_reduce_fusion.2
  64.3 1.3 select_reduce_fusion.1
  66.3 1.3 select_reduce_fusion
  68.0 6.2 %fusion.83 = f32[512,512]{0,1:S(1)} fusion(bf16[512,4096]{1,0:T(8,128)(2,1)} %copy-done.2, bf16[4096,512]{0,1:T(8,128)(2,1)} %bitcast.164), kind=kOutput, calls=%fused_computation.120 | convolution fusion | flops 2147483648 | bytes 9437184
  75.2 1.3 collective-permute-start
  76.5 2.4 collective-permute-start.2
  78.9 6.7 %fusion.40 = bf16[512,4,128]{2,0,1:T(8,128)(2,1)} fusion(bf16[4096,4,128]{2,0,1:T(8,128)(2,1)} %all-gather.6.cloned.1.call-done, bf16[512,4096]{1,0:T(8,128)(2,1)} %copy-done.2), kind=kOutput, calls=%fused_computation.49 | convolution fusion | flops 2147745792 | bytes 8912896 | tf_op jit(solution)/shard_map/td,dgh->tgh/dot_general | solution.py:60
  86.9 2.4 collective-permute-start.3
  89.3 7.3 %fusion.3 = f32[512,4,256]{0,2,1:T(8,128)S(1)} fusion(bf16[4096,4,256]{2,1,0:T(4,128)(2,1)} %param.8, bf16[512,4096]{1,0:T(8,128)(2,1)S(1)} %copy-done.3), kind=kOutput, calls=%fused_computation.7 | convolution fusion | flops 4294967296 | bytes 14680064 | tf_op jit(solution)/shard_map/td,dgc->tgc/dot_general | solution.py:50
  96.8 2.0 copy.74
  98.8 1.9 copy.75
  100.7 2.9 %subtract_convert_fusion = (bf16[512,4,2,64]{3,0,2,1:T(8,128)(2,1)S(1)}, bf16[512,4,2,64]{3,0,2,1:T(8,128)(2,1)S(1)}) fusion(f32[512,4,2,64]{3,0,2,1:T(8,128)} %copy.75, f32[512,4,2,64]{3,0,2,1:T(8,128)} %copy.74, f32[512,64]{1,0:T(8,128)S(1)} %copy.36, f32[512,64]{1,0:T(8,128)S(1)} %copy.34), kind=kLoop, calls=%fused_computation.43 | loop fusion | flops 2097152 | bytes 3407872 | tf_op jit(solution)/shard_map/convert.4
  103.6 2.3 fusion.7
  106.0 1.8 fusion.5
  107.7 1.5 copy-done.1
  109.2 20.5 %collective-permute-done = bf16[512,4,128]{0,2,1:T(8,128)(2,1)} collective-permute-done((bf16[512,4,128]{0,2,1:T(8,128)(2,1)}, bf16[512,4,128]{0,2,1:T(8,128)(2,1)}, u32[]{:S(2)}, u32[]{:S(2)}) %collective-permute-start) | collective-permute-done | bytes 524320 | tf_op jit(solution)/shard_map/ppermute | solution.py:18
  129.7 1.3 copy.65
  131.0 1.3 copy.70
  135.7 28.4 %collective-permute-done.1 = bf16[512,4,128]{2,0,1:T(8,128)(2,1)} collective-permute-done((bf16[512,4,128]{2,0,1:T(8,128)(2,1)}, bf16[512,4,128]{2,0,1:T(8,128)(2,1)}, u32[]{:S(2)}, u32[]{:S(2)}) %collective-permute-start.1) | collective-permute-done | bytes 524320 | tf_op jit(solution)/shard_map/ppermute | solution.py:18
  164.0 1.5 fusion.34
  166.8 1.9 fusion.37
  169.8 3.5 %fusion.31 = bf16[512,4,2,128]{0,3,2,1:T(8,128)(2,1)S(1)} fusion(f32[512,4,2,128]{0,3,2,1:T(8,128)S(1)} %bitcast.155, f32[512,4,2,128]{0,3,2,1:T(8,128)S(1)} %bitcast.154, f32[4,512,512,2]{2,1,3,0:T(8,128)S(1)} %bitcast.151, f32[4,2,512]{2,1,0:T(2,128)S(1)} %get-tuple-element.34, pred[512,512]{0,1:T(8,128)(4,1)S(1)} %fusion.48, ...), kind=kOutput, calls=%fused_computation.44 | convolution fusion | flops 548405248 | bytes 14483456 | tf_op jit(solution)/shard_map/grtu,ugh->tgrh/dot_general | solution.py:81
  173.3 1.4 copy.51
  174.7 84.6 %reduce-scatter.2.cloned.1.call-done = bf16[1024,1024]{1,0:T(8,128)(2,1)} async-done(((bf16[4096,1024]{1,0:T(8,128)(2,1)}), bf16[1024,1024]{1,0:T(8,128)(2,1)}) %reduce-scatter.2.cloned.1.call-update) | async-done | bytes 2097168 | tf_op jit(solution)/shard_map/reduce_scatter | solution.py:119
  259.4 4.1 %convert_element_type.49 = f32[1024,1024]{1,0:T(8,128)} convert(bf16[1024,1024]{1,0:T(8,128)(2,1)} %reduce-scatter.2.cloned.1.call-done) | non-fusion elementwise | flops 1048576 | bytes 6291456 | tf_op jit(solution)/shard_map/convert_element_type | solution.py:127
  (57 shorter events, 12.4 us)
Async XLA Ops:
  7.2 5.2 %copy-start.4 = (bf16[2048,4,128]{2,1,0:T(4,128)(2,1)S(1)}, bf16[2048,4,128]{2,1,0:T(4,128)(2,1)}, u32[]{:S(2)}) copy-start(bf16[2048,4,128]{2,1,0:T(4,128)(2,1)} %param.10) | copy-start | bytes 6291460
  7.2 39.6 %all-gather.4.cloned.1.call-start = ((), (), s32[]{:S(2)}) async-start(), calls=%async_computation.1 | async-start | bytes 5242880 | tf_op jit(solution)/shard_map/all_gather | solution.py:37
  7.9 60.0 %all-gather.8.cloned.1.call-start = ((), (), s32[]{:S(2)}) async-start(), calls=%async_computation.3 | async-start | bytes 6291456 | tf_op jit(solution)/shard_map/all_gather | solution.py:57
  12.3 66.6 %all-gather.6.cloned.1.call-start = ((), (), s32[]{:S(2)}) async-start(), calls=%async_computation.2 | async-start | bytes 6291456 | tf_op jit(solution)/shard_map/all_gather | solution.py:63
  14.0 36.0 %copy-start.5 = (f32[4096]{0:T(1024)S(1)}, f32[4096]{0:T(1024)}, u32[]{:S(2)}) copy-start(f32[4096]{0:T(1024)} %param.7) | copy-start | bytes 49156
  14.0 245.3 %reduce-scatter.2.cloned.1.call-start = ((), (), s32[]{:S(2)}) async-start(), calls=%async_computation.4 | async-start | bytes 10485760 | tf_op jit(solution)/shard_map/reduce_scatter | solution.py:119
  46.8 3.4 %copy-start = (bf16[512,4096]{1,0:T(8,128)(2,1)S(1)}, bf16[512,4096]{1,0:T(8,128)(2,1)}, u32[]{:S(2)}) copy-start(bf16[512,4096]{1,0:T(8,128)(2,1)} %all-gather.4.cloned.1.call-done) | copy-start | bytes 12582916
  51.8 2.0 copy-start.2
  60.8 0.9 copy-start.6
  75.2 54.5 %collective-permute-start = (bf16[512,4,128]{0,2,1:T(8,128)(2,1)}, bf16[512,4,128]{0,2,1:T(8,128)(2,1)}, u32[]{:S(2)}, u32[]{:S(2)}) collective-permute-start(bf16[512,4,128]{0,2,1:T(8,128)(2,1)} %pad_maximum_fusion.1), channel_id=1, source_target_pairs={{0,4},{4,0},{8,12},{12,8},{1,5},{5,1},{9,13},{13,9},{2,6},{6,2},{1... | collective-permute-start | bytes 1572872 | tf_op jit(solution)/shard_map/ppermute | solution.py:18
  76.5 54.5 %collective-permute-start.2 = (bf16[512,4,128]{0,2,1:T(8,128)(2,1)}, bf16[512,4,128]{0,2,1:T(8,128)(2,1)}, u32[]{:S(2)}, u32[]{:S(2)}) collective-permute-start(bf16[512,4,128]{0,2,1:T(8,128)(2,1)} %pad_maximum_fusion.1), channel_id=1, source_target_pairs={{0,8},{8,0},{4,12},{12,4},{1,9},{9,1},{5,13},{13,5},{2,10},{10,2},... | collective-permute-start | bytes 1572872 | tf_op jit(solution)/shard_map/ppermute | solution.py:18
  78.9 10.4 %copy-start.3 = (bf16[512,4096]{1,0:T(8,128)(2,1)S(1)}, bf16[512,4096]{1,0:T(8,128)(2,1)}, u32[]{:S(2)}) copy-start(bf16[512,4096]{1,0:T(8,128)(2,1)} %copy-done.2) | copy-start | bytes 12582916
  85.6 78.4 %collective-permute-start.1 = (bf16[512,4,128]{2,0,1:T(8,128)(2,1)}, bf16[512,4,128]{2,0,1:T(8,128)(2,1)}, u32[]{:S(2)}, u32[]{:S(2)}) collective-permute-start(bf16[512,4,128]{2,0,1:T(8,128)(2,1)} %fusion.40), channel_id=1, source_target_pairs={{0,4},{4,0},{8,12},{12,8},{1,5},{5,1},{9,13},{13,9},{2,6},{6,2},{1... | collective-permute-start | bytes 1572872 | tf_op jit(solution)/shard_map/ppermute | solution.py:18
  86.9 79.9 %collective-permute-start.3 = (bf16[512,4,128]{2,0,1:T(8,128)(2,1)}, bf16[512,4,128]{2,0,1:T(8,128)(2,1)}, u32[]{:S(2)}, u32[]{:S(2)}) collective-permute-start(bf16[512,4,128]{2,0,1:T(8,128)(2,1)} %fusion.40), channel_id=1, source_target_pairs={{0,8},{8,0},{4,12},{12,4},{1,9},{9,1},{5,13},{13,5},{2,10},{10,2},... | collective-permute-start | bytes 1572872 | tf_op jit(solution)/shard_map/ppermute | solution.py:18
  105.9 3.2 %copy-start.1 = (f32[4,512,512,2]{2,1,3,0:T(8,128)}, f32[4,512,512,2]{2,1,3,0:T(8,128)S(1)}, u32[]{:S(2)}) copy-start(f32[4,512,512,2]{2,1,3,0:T(8,128)S(1)} %get-tuple-element.35) | copy-start | bytes 25165828
  165.8 3.2 %slice-start = ((s8[8388608]{0:T(1024)(128)(4,1)}), s8[4194304]{0:T(1024)(128)(4,1)S(1)}, s32[]{:S(2)}) async-start(s8[8388608]{0:T(1024)(128)(4,1)} %bitcast.150), calls=%async_computation.5 | async-start | bytes 8388608
  166.8 3.0 %slice-start.1 = ((s8[8388608]{0:T(1024)(128)(4,1)}), s8[4194304]{0:T(1024)(128)(4,1)S(1)}, s32[]{:S(2)}) async-start(s8[8388608]{0:T(1024)(128)(4,1)} %bitcast.150), calls=%async_computation.6 | async-start | bytes 8388608
Sparse Core Ops, SparseCore 0:
  9.5 37.1 all-gather.3
  48.3 13.6 all-gather.7
  63.6 14.8 all-gather.5
  80.6 178.6 reduce-scatter.1
where the time goes:
time: 270 us
  waiting for transfers between devices  167 us (62%)
  matrix products  38.8 us (14%)
  other arithmetic  21.5 us (8%)
  local copies, waits for them, and re-layouts  21.2 us (8%)
  between operations  14 us (5%)
  starting transfers between devices  7.57 us (3%)
    reduce_scatter x1, waiting for transfers between devices, body(): lax.psum_scatter((jnp.einsum('tc,tr->cr', normed, owned, preferred_elemen...  84.6 us
    ppermute x4, waiting for transfers between devices, from_partner(): return lax.ppermute(block, axis, route)  48.8 us
    all_gather x1, waiting for transfers between devices, body(): gathered = lax.all_gather(tokens, ('kvh', 'sub'), axis=1, tiled=True)  32.7 us
    unnamed x23, local copies, waits for them, and re-layouts  15.7 us
    ppermute x4, starting transfers between devices, from_partner(): return lax.ppermute(block, axis, route)  7.41 us
    dot_general x1, matrix products, body(): jnp.einsum('td,dgc->tgc', normed, w_query, preferred_element_type=jnp.flo...  7.28 us
    dot_general x1, matrix products, body(): jnp.einsum('tc,tr->cr', normed, owned, preferred_element_type=jnp.float32)  6.98 us
    dot_general x1, matrix products, body(): jnp.einsum('td,dgh->tgh', normed, lax.all_gather(w_value, 'sub', axis=0,...  6.73 us
  transfers between devices with their start and end apart: 8, of which 4 were waited for; matrix products, arithmetic and copies ran while one was open for 27% of the time, Pallas kernels for 0%

commit v1 on v0

--- a/solution.py
+++ b/solution.py
@@ -51,18 +51,23 @@
     queries = rotate(
         queries.reshape(row_count, local_groups, per_group, head_size), positions
     ).astype(jnp.bfloat16)
-    key_more = jnp.einsum(
-        "td,dgh->tgh",
-        normed,
-        lax.all_gather(w_key, "sub", axis=0, tiled=True),
-        preferred_element_type=jnp.float32,
-    )
-    value_more = jnp.einsum(
-        "td,dgh->tgh",
-        normed,
-        lax.all_gather(w_value, "sub", axis=0, tiled=True),
-        preferred_element_type=jnp.float32,
-    )
+    sub_count = lax.axis_size("sub")
+    sub_index = lax.axis_index("sub")
+    row_share = w_key.shape[0]
+    key_more = None
+    value_more = None
+    for shift in range(sub_count):
+        if shift == 0:
+            key_part, value_part = w_key, w_value
+        else:
+            route = [(j, (j + shift) % sub_count) for j in range(sub_count)]
+            key_part, value_part = lax.ppermute((w_key, w_value), "sub", route)
+        source = (sub_index - shift) % sub_count
+        rows = lax.dynamic_slice_in_dim(normed, source * row_share, row_share, 1)
+        key_step = jnp.einsum("td,dgh->tgh", rows, key_part, preferred_element_type=jnp.float32)
+        value_step = jnp.einsum("td,dgh->tgh", rows, value_part, preferred_element_type=jnp.float32)
+        key_more = key_step if key_more is None else key_more + key_step
+        value_more = value_step if value_more is None else value_more + value_step
     keys = rotate(key_more, positions).astype(jnp.bfloat16)
     values = value_more.astype(jnp.bfloat16)
     block_ids = seq_index * 2 + jnp.arange(2, dtype=jnp.int32)
@@ -115,16 +120,22 @@
     owner_index = lax.axis_index("kvh") * lax.axis_size("sub") + lax.axis_index("sub")
     owned = lax.dynamic_slice_in_dim(normed, owner_index * tile_cols, tile_cols, 1)
     seq_count = lax.axis_size("seq")
+    band = width // seq_count
     inverse_count = 1.0 / (row_count * seq_count)
-    gram_tile = lax.psum_scatter(
-        (
-            jnp.einsum("tc,tr->cr", normed, owned, preferred_element_type=jnp.float32)
-            * inverse_count
-        ).astype(jnp.bfloat16),
-        "seq",
-        scatter_dimension=0,
-        tiled=True,
-    ).astype(jnp.float32)
+    all_owned = lax.all_gather(owned, "seq", axis=0, tiled=True)
+    mine = lax.dynamic_slice_in_dim(normed, seq_index * band, band, 1)
+    gram_sum = jnp.einsum("tc,tr->cr", mine, owned, preferred_element_type=jnp.float32)
+    for shift in range(1, seq_count):
+        target = (seq_index + shift) % seq_count
+        outgoing = lax.dynamic_slice_in_dim(normed, target * band, band, 1)
+        route = [(j, (j + shift) % seq_count) for j in range(seq_count)]
+        incoming = lax.ppermute(outgoing, "seq", route)
+        source = (seq_index - shift) % seq_count
+        their_owned = lax.dynamic_slice_in_dim(all_owned, source * row_count, row_count, 0)
+        gram_sum = gram_sum + jnp.einsum(
+            "tc,tr->cr", incoming, their_owned, preferred_element_type=jnp.float32
+        )
+    gram_tile = gram_sum * inverse_count
     return (attended, gram_tile)
 
 

time: 270 us -> 277 us (1.026)
  the two profiles are of different devices: /device:TPU:0 before, /device:TPU:21 now
where the time goes in v1:
time: 277 us
  waiting for transfers between devices  167 us (60%)
  matrix products  44.4 us (16%)
  local copies, waits for them, and re-layouts  22.9 us (8%)
  other arithmetic  15.4 us (6%)
  between operations  14.5 us (5%)
  starting transfers between devices  12.2 us (4%)
    ppermute x3, waiting for transfers between devices, body(): incoming = lax.ppermute(outgoing, 'seq', route)  124 us
    all_gather x1, waiting for transfers between devices, body(): gathered = lax.all_gather(tokens, ('kvh', 'sub'), axis=1, tiled=True)  22.4 us
    ppermute x4, waiting for transfers between devices, from_partner(): return lax.ppermute(block, axis, route)  20.6 us
    unnamed x45, local copies, waits for them, and re-layouts  13.9 us
    dot_general x3, matrix products, body(): jnp.einsum('tc,tr->cr', incoming, their_owned, preferred_element_type=jnp...  10.6 us
    dot_general x1, matrix products, body(): jnp.einsum('td,dgc->tgc', normed, w_query, preferred_element_type=jnp.flo...  8.46 us
    ppermute x3, starting transfers between devices, body(): incoming = lax.ppermute(outgoing, 'seq', route)  7.65 us
  transfers between devices with their start and end apart: 11, of which 4 were waited for; matrix products, arithmetic and copies ran while one was open for 27% of the time, Pallas kernels for 0%

profile of v1, /device:TPU:21, one launch (start us, length us, event | category | flops | bytes accessed | tf_op | source)
XLA Modules:
  0.0 276.8 jit_solution(10976070409066014879)
XLA Ops:
  8.0 4.4 %copy.34 = bf16[2048,4,128]{0,2,1:T(8,128)(2,1)} copy(bf16[2048,4,128]{2,1,0:T(4,128)(2,1)} %param.9) | data formatting | bytes 4194304 | tf_op args[3]
  13.0 1.6 copy.32
  15.3 1.3 select_reduce_fusion
  18.8 1.3 select_reduce_fusion.1
  23.1 22.4 %all-gather.3.cloned.1.call-done = bf16[512,4096]{1,0:T(8,128)(2,1)} async-done(((bf16[512,1024]{1,0:T(8,128)(2,1)}), bf16[512,4096]{1,0:T(8,128)(2,1)}) %all-gather.3.cloned.1.call-update) | async-done | bytes 4194320 | tf_op jit(solution)/shard_map/all_gather | solution.py:37
  45.5 3.2 %fusion = f32[512]{0:T(512)S(1)} fusion(bf16[512,4096]{1,0:T(8,128)(2,1)} %all-gather.3.cloned.1.call-done), kind=kLoop, calls=%fused_computation.2 | loop fusion | flops 6290944 | bytes 4196352 | tf_op jit(solution)/shard_map/reduce_sum | solution.py:39
  49.0 1.7 fusion.2
  50.7 1.3 fusion.37
  52.0 2.9 %fusion.34 = f32[512,512]{0,1:S(1)} fusion(bf16[2048,512]{0,1:T(8,128)(2,1)} %bitcast.8, bf16[512,4096]{1,0:T(8,128)(2,1)S(1)} %fusion.2, s32[]{:T(128)S(6)} %select_n.127), kind=kOutput, calls=%fused_computation.47 | convolution fusion | flops 1073741824 | bytes 5242884
  58.9 3.7 %fusion.51 = bf16[512,4,128]{2,0,1:T(8,128)(2,1)} fusion(f32[512,4,128]{2,0,1:T(8,128)S(1)} %fusion.31, bf16[2048,4,128]{2,0,1:T(8,128)(2,1)} %collective-permute-done, bf16[512,4096]{1,0:T(8,128)(2,1)S(1)} %fusion.2, s32[]{:T(128)S(6)} %select_n.127), kind=kOutput, calls=%fused_computation.58 | convolution fusion | flops 1074266112 | bytes 5767172 | tf_op jit(solution)/shard_map/td,dgh->tgh/dot_general | solution.py:68
  62.6 2.2 collective-permute-start.5
  65.0 2.1 constant_dynamic-slice_fusion
  67.2 8.5 %fusion.3 = f32[512,4,256]{0,2,1:T(8,128)S(1)} fusion(bf16[4096,4,256]{2,1,0:T(4,128)(2,1)} %param.8, bf16[512,4096]{1,0:T(8,128)(2,1)} %copy-done), kind=kOutput, calls=%fused_computation.6 | convolution fusion | flops 4294967296 | bytes 14680064 | tf_op jit(solution)/shard_map/td,dgc->tgc/dot_general | solution.py:50
  75.8 1.9 copy.79
  77.8 1.9 copy.78
  80.0 4.6 %fusion.66 = f32[1024,1024]{1,0:T(8,128)} fusion(bf16[512,1024]{1,0:T(8,128)(2,1)S(1)} %copy-done.5, bf16[512,4096]{1,0:T(8,128)(2,1)} %copy-done, s32[]{:T(128)S(6)} %select_n.135), kind=kOutput, calls=%fused_computation.70 | convolution fusion | flops 1073741824 | bytes 6291460 | tf_op jit(solution)/shard_map/tc,tr->cr/dot_general | solution.py:127
  85.6 2.3 fusion.7
  88.0 1.8 fusion.5
  89.8 1.5 copy-done.2
  91.2 7.1 %collective-permute-start.6 = (bf16[512,1024]{1,0:T(8,128)(2,1)}, bf16[512,1024]{1,0:T(8,128)(2,1)}, u32[]{:S(2)}, u32[]{:S(2)}) collective-permute-start(bf16[512,1024]{1,0:T(8,128)(2,1)} %get-tuple-element.19), channel_id=1, source_target_pairs={{0,4},{4,8},{8,12},{12,0},{1,5},{5,9},{9,13},{13,1},{2,6},{6,10},{... | collective-permute-start | bytes 3145736 | tf_op jit(solution)/shard_map/ppermute | solution.py:132
  98.4 1.3 copy.74
  100.0 1.3 copy.69
  104.7 20.5 %collective-permute-done.5 = bf16[512,4,128]{2,0,1:T(8,128)(2,1)} collective-permute-done((bf16[512,4,128]{2,0,1:T(8,128)(2,1)}, bf16[512,4,128]{2,0,1:T(8,128)(2,1)}, u32[]{:S(2)}, u32[]{:S(2)}) %collective-permute-start.5) | collective-permute-done | bytes 524320 | tf_op jit(solution)/shard_map/ppermute | solution.py:18
  125.2 1.5 fusion.45
  127.8 1.8 fusion.42
  130.6 3.5 %fusion.33 = bf16[512,4,2,128]{0,3,2,1:T(8,128)(2,1)S(1)} fusion(f32[512,4,2,128]{0,3,2,1:T(8,128)S(1)} %bitcast.166, f32[512,4,2,128]{0,3,2,1:T(8,128)S(1)} %bitcast.167, f32[4,512,512,2]{2,1,3,0:T(8,128)S(1)} %bitcast.162, f32[4,2,512]{2,1,0:T(2,128)S(1)} %get-tuple-element.38, pred[512,512]{0,1:T(8,128)(4,1)S(1)} %fusion.68, ...), kind=kOutput, calls=%fused_computation.46 | convolution fusion | flops 548405248 | bytes 14483456 | tf_op jit(solution)/shard_map/grtu,ugh->tgrh/dot_general | solution.py:86
  134.1 1.4 copy.55
  135.6 100.7 %collective-permute-done.7 = bf16[512,1024]{1,0:T(8,128)(2,1)} collective-permute-done((bf16[512,1024]{1,0:T(8,128)(2,1)}, bf16[512,1024]{1,0:T(8,128)(2,1)}, u32[]{:S(2)}, u32[]{:S(2)}) %collective-permute-start.7) | collective-permute-done | bytes 1048608 | tf_op jit(solution)/shard_map/ppermute | solution.py:132
  236.3 3.0 %fusion.62 = f32[1024,1024]{1,0:T(8,128)S(1)} fusion(bf16[512,1024]{1,0:T(8,128)(2,1)} %collective-permute-done.7, bf16[2048,1024]{1,0:T(8,128)(2,1)} %all-gather.5.cloned.1.call-done, s32[]{:T(128)S(6)} %select_n.144), kind=kOutput, calls=%fused_computation.66 | convolution fusion | flops 1073741824 | bytes 6291460 | tf_op jit(solution)/shard_map/tc,tr->cr/dot_general | solution.py:135
  239.3 23.1 %collective-permute-done.6 = bf16[512,1024]{1,0:T(8,128)(2,1)} collective-permute-done((bf16[512,1024]{1,0:T(8,128)(2,1)}, bf16[512,1024]{1,0:T(8,128)(2,1)}, u32[]{:S(2)}, u32[]{:S(2)}) %collective-permute-start.6) | collective-permute-done | bytes 1048608 | tf_op jit(solution)/shard_map/ppermute | solution.py:132
  262.4 2.5 fusion.64
  264.9 5.0 %add_multiply_fusion = f32[1024,1024]{1,0:T(8,128)} fusion(f32[1024,1024]{1,0:T(8,128)S(1)} %fusion.62, f32[1024,1024]{1,0:T(8,128)S(1)} %copy-done.6, f32[1024,1024]{1,0:T(8,128)S(1)} %fusion.64, bf16[512,1024]{1,0:T(8,128)(2,1)} %collective-permute-done.8, bf16[2048,1024]{1,0:T(8,128)(2,1)S(1)} %copy-done.7, s32[]{:T(128)S(6)} %select_n.148), kind=kOutput, calls=%fused_computation.20 | convolution fusion | flops 1077936128 | bytes 18874372 | tf_op jit(solution)/shard_map/tc,tr->cr/dot_general | solution.py:135
  (89 shorter events, 18.8 us)
Async XLA Ops:
  7.2 5.9 %copy-start.8 = (bf16[2048,4,128]{2,1,0:T(4,128)(2,1)S(1)}, bf16[2048,4,128]{2,1,0:T(4,128)(2,1)}, u32[]{:S(2)}) copy-start(bf16[2048,4,128]{2,1,0:T(4,128)(2,1)} %param.10) | copy-start | bytes 6291460
  7.2 38.3 %all-gather.3.cloned.1.call-start = ((), (), s32[]{:S(2)}) async-start(), calls=%async_computation | async-start | bytes 5242880 | tf_op jit(solution)/shard_map/all_gather | solution.py:37
  7.9 6.8 %copy-start.17 = (s32[3,8]{1,0:T(4,128)S(1)}, s32[3,8]{1,0:T(4,128)}, u32[]{:S(2)}) copy-start(s32[3,8]{1,0:T(4,128)} %param.11) | copy-start | bytes 292
  7.9 228.4 %all-gather.5.cloned.1.call-start = ((), (), s32[]{:S(2)}) async-start(), calls=%async_computation.1 | async-start | bytes 5242880 | tf_op jit(solution)/shard_map/all_gather | solution.py:125
  12.3 36.4 %copy-start.16 = (f32[4096]{0:T(1024)S(1)}, f32[4096]{0:T(1024)}, u32[]{:S(2)}) copy-start(f32[4096]{0:T(1024)} %param.7) | copy-start | bytes 49156
  12.3 39.6 %collective-permute-start.1 = (bf16[2048,4,128]{0,2,1:T(8,128)(2,1)}, bf16[2048,4,128]{0,2,1:T(8,128)(2,1)}, u32[]{:S(2)}, u32[]{:S(2)}) collective-permute-start(bf16[2048,4,128]{0,2,1:T(8,128)(2,1)} %copy.34), channel_id=1, source_target_pairs={{0,1},{1,0},{2,3},{3,2},{4,5},{5,4},{6,7},{7,6},{8,9},{9,8},{10,11... | collective-permute-start | bytes 6291464 | tf_op jit(solution)/shard_map/ppermute | solution.py:64
  14.7 44.2 %collective-permute-start = (bf16[2048,4,128]{2,0,1:T(8,128)(2,1)}, bf16[2048,4,128]{2,0,1:T(8,128)(2,1)}, u32[]{:S(2)}, u32[]{:S(2)}) collective-permute-start(bf16[2048,4,128]{2,0,1:T(8,128)(2,1)} %copy.32), channel_id=1, source_target_pairs={{0,1},{1,0},{2,3},{3,2},{4,5},{5,4},{6,7},{7,6},{8,9},{9,8},{10,11... | collective-permute-start | bytes 6291464 | tf_op jit(solution)/shard_map/ppermute | solution.py:64
  45.5 3.4 %copy-start.1 = (bf16[512,4096]{1,0:T(8,128)(2,1)S(1)}, bf16[512,4096]{1,0:T(8,128)(2,1)}, u32[]{:S(2)}) copy-start(bf16[512,4096]{1,0:T(8,128)(2,1)} %all-gather.3.cloned.1.call-done) | copy-start | bytes 12582916
  49.0 1.7 copy-start.9
  50.6 14.4 %copy-start = (bf16[512,4096]{1,0:T(8,128)(2,1)}, bf16[512,4096]{1,0:T(8,128)(2,1)S(1)}, u32[]{:S(2)}) copy-start(bf16[512,4096]{1,0:T(8,128)(2,1)S(1)} %fusion.2) | copy-start | bytes 12582916
  55.3 3.6 %copy-start.10 = (bf16[512,4,64]{0,2,1:T(8,128)(2,1)}, bf16[512,4,64]{0,2,1:T(8,128)(2,1)S(1)}, u32[]{:S(2)}) copy-start(bf16[512,4,64]{0,2,1:T(8,128)(2,1)S(1)} %get-tuple-element.23) | copy-start | bytes 786436
  55.3 3.6 %copy-start.12 = (bf16[512,4,64]{0,2,1:T(8,128)(2,1)}, bf16[512,4,64]{0,2,1:T(8,128)(2,1)S(1)}, u32[]{:S(2)}) copy-start(bf16[512,4,64]{0,2,1:T(8,128)(2,1)S(1)} %get-tuple-element.24) | copy-start | bytes 786436
  56.2 35.0 %collective-permute-start.4 = (bf16[512,4,128]{0,2,1:T(8,128)(2,1)}, bf16[512,4,128]{0,2,1:T(8,128)(2,1)}, u32[]{:S(2)}, u32[]{:S(2)}) collective-permute-start(bf16[512,4,128]{0,2,1:T(8,128)(2,1)} %pad_maximum_fusion.1), channel_id=1, source_target_pairs={{0,8},{8,0},{4,12},{12,4},{1,9},{9,1},{5,13},{13,5},{2,10},{10,2},... | collective-permute-start | bytes 1572872 | tf_op jit(solution)/shard_map/ppermute | solution.py:18
  56.4 43.3 %collective-permute-start.2 = (bf16[512,4,128]{0,2,1:T(8,128)(2,1)}, bf16[512,4,128]{0,2,1:T(8,128)(2,1)}, u32[]{:S(2)}, u32[]{:S(2)}) collective-permute-start(bf16[512,4,128]{0,2,1:T(8,128)(2,1)} %pad_maximum_fusion.1), channel_id=1, source_target_pairs={{0,4},{4,0},{8,12},{12,8},{1,5},{5,1},{9,13},{13,9},{2,6},{6,2},{1... | collective-permute-start | bytes 1572872 | tf_op jit(solution)/shard_map/ppermute | solution.py:18
  62.6 62.6 %collective-permute-start.5 = (bf16[512,4,128]{2,0,1:T(8,128)(2,1)}, bf16[512,4,128]{2,0,1:T(8,128)(2,1)}, u32[]{:S(2)}, u32[]{:S(2)}) collective-permute-start(bf16[512,4,128]{2,0,1:T(8,128)(2,1)} %fusion.51), channel_id=1, source_target_pairs={{0,8},{8,0},{4,12},{12,4},{1,9},{9,1},{5,13},{13,5},{2,10},{10,2},... | collective-permute-start | bytes 1572872 | tf_op jit(solution)/shard_map/ppermute | solution.py:18
  64.7 63.0 %collective-permute-start.3 = (bf16[512,4,128]{2,0,1:T(8,128)(2,1)}, bf16[512,4,128]{2,0,1:T(8,128)(2,1)}, u32[]{:S(2)}, u32[]{:S(2)}) collective-permute-start(bf16[512,4,128]{2,0,1:T(8,128)(2,1)} %fusion.51), channel_id=1, source_target_pairs={{0,4},{4,0},{8,12},{12,8},{1,5},{5,1},{9,13},{13,9},{2,6},{6,2},{1... | collective-permute-start | bytes 1572872 | tf_op jit(solution)/shard_map/ppermute | solution.py:18
  75.8 4.1 %copy-start.5 = (bf16[512,1024]{1,0:T(8,128)(2,1)S(1)}, bf16[512,1024]{1,0:T(8,128)(2,1)}, u32[]{:S(2)}) copy-start(bf16[512,1024]{1,0:T(8,128)(2,1)} %get-tuple-element.20) | copy-start | bytes 3145732
  79.7 4.9 %copy-start.3 = (f32[512,4,2,64]{3,0,2,1:T(8,128)S(1)}, f32[512,4,2,64]{3,0,2,1:T(8,128)}, u32[]{:S(2)}) copy-start(f32[512,4,2,64]{3,0,2,1:T(8,128)} %copy.79) | copy-start | bytes 3145732
  79.7 4.9 %copy-start.4 = (f32[512,4,2,64]{3,0,2,1:T(8,128)S(1)}, f32[512,4,2,64]{3,0,2,1:T(8,128)}, u32[]{:S(2)}) copy-start(f32[512,4,2,64]{3,0,2,1:T(8,128)} %copy.78) | copy-start | bytes 3145732
  79.7 4.9 %copy-start.14 = (f32[512,64]{1,0:T(8,128)S(1)}, f32[512,64]{1,0:T(8,128)}, u32[]{:S(2)}) copy-start(f32[512,64]{1,0:T(8,128)} %copy.40) | copy-start | bytes 393220
  79.7 4.9 %copy-start.15 = (f32[512,64]{1,0:T(8,128)S(1)}, f32[512,64]{1,0:T(8,128)}, u32[]{:S(2)}) copy-start(f32[512,64]{1,0:T(8,128)} %copy.38) | copy-start | bytes 393220
  79.7 156.6 %collective-permute-start.7 = (bf16[512,1024]{1,0:T(8,128)(2,1)}, bf16[512,1024]{1,0:T(8,128)(2,1)}, u32[]{:S(2)}, u32[]{:S(2)}) collective-permute-start(bf16[512,1024]{1,0:T(8,128)(2,1)} %get-tuple-element.18), channel_id=1, source_target_pairs={{0,8},{4,12},{8,0},{12,4},{1,9},{5,13},{9,1},{13,5},{2,10},{6,14},... | collective-permute-start | bytes 3145736 | tf_op jit(solution)/shard_map/ppermute | solution.py:132
  84.6 1.0 copy-start.11
  84.6 1.0 copy-start.13
  88.0 3.2 %copy-start.2 = (f32[4,512,512,2]{2,1,3,0:T(8,128)}, f32[4,512,512,2]{2,1,3,0:T(8,128)S(1)}, u32[]{:S(2)}) copy-start(f32[4,512,512,2]{2,1,3,0:T(8,128)S(1)} %get-tuple-element.39) | copy-start | bytes 25165828
  91.2 171.1 %collective-permute-start.6 = (bf16[512,1024]{1,0:T(8,128)(2,1)}, bf16[512,1024]{1,0:T(8,128)(2,1)}, u32[]{:S(2)}, u32[]{:S(2)}) collective-permute-start(bf16[512,1024]{1,0:T(8,128)(2,1)} %get-tuple-element.19), channel_id=1, source_target_pairs={{0,4},{4,8},{8,12},{12,0},{1,5},{5,9},{9,13},{13,1},{2,6},{6,10},{... | collective-permute-start | bytes 3145736 | tf_op jit(solution)/shard_map/ppermute | solution.py:132
  99.7 165.2 %collective-permute-start.8 = (bf16[512,1024]{1,0:T(8,128)(2,1)}, bf16[512,1024]{1,0:T(8,128)(2,1)}, u32[]{:S(2)}, u32[]{:S(2)}) collective-permute-start(bf16[512,1024]{1,0:T(8,128)(2,1)} %get-tuple-element.17), channel_id=1, source_target_pairs={{0,12},{4,0},{8,4},{12,8},{1,13},{5,1},{9,5},{13,9},{2,14},{6,2},{... | collective-permute-start | bytes 3145736 | tf_op jit(solution)/shard_map/ppermute | solution.py:132
  126.7 3.4 %slice-start = ((s8[8388608]{0:T(1024)(128)(4,1)}), s8[4194304]{0:T(1024)(128)(4,1)S(1)}, s32[]{:S(2)}) async-start(s8[8388608]{0:T(1024)(128)(4,1)} %bitcast.161), calls=%async_computation.2 | async-start | bytes 8388608
  127.7 2.9 %slice-start.1 = ((s8[8388608]{0:T(1024)(128)(4,1)}), s8[4194304]{0:T(1024)(128)(4,1)S(1)}, s32[]{:S(2)}) async-start(s8[8388608]{0:T(1024)(128)(4,1)} %bitcast.161), calls=%async_computation.3 | async-start | bytes 8388608
  236.3 26.1 %copy-start.7 = (bf16[2048,1024]{1,0:T(8,128)(2,1)S(1)}, bf16[2048,1024]{1,0:T(8,128)(2,1)}, u32[]{:S(2)}) copy-start(bf16[2048,1024]{1,0:T(8,128)(2,1)} %all-gather.5.cloned.1.call-done) | copy-start | bytes 12582916
  239.3 25.6 %copy-start.6 = (f32[1024,1024]{1,0:T(8,128)S(1)}, f32[1024,1024]{1,0:T(8,128)}, u32[]{:S(2)}) copy-start(f32[1024,1024]{1,0:T(8,128)} %fusion.66) | copy-start | bytes 12582916
Sparse Core Ops, SparseCore 0:
  9.5 35.9 all-gather.2
  67.3 167.9 all-gather.4
